TPU v7x, 128 devices: a whole 4x4x4 slice. The times are simulated.
128 devices in a mesh: req: 32 (over z, x, core), tok: 4 (over y).
Axes of the slice: x: 4, y: 4, z: 4, core: 2. Of those that a mesh axis runs over, the one named last changes fastest.
Arguments:
- tokens: bfloat16 [32768, 1280], P(('req', 'tok')), may hold values from -6 to 6
- segments: int32 [32, 1024], P('req'), may hold values from 0 to 16, as said below
- gain_attn: float32 [1280], replicated, may hold values from 0.1 to 1.9
- w_qkv: bfloat16 [1280, 3, 1280], P(None, None, 'tok'), may hold values from -1 to 1
- w_out: bfloat16 [1280, 1280], P('tok'), may hold values from -0.15625 to 0.15625
- gain_mlp: float32 [1280], replicated, may hold values from 0.1 to 1.9
- w_up: bfloat16 [1280, 5120], P(None, ('req', 'tok')), may hold values from -0.15625 to 0.15625
- w_down_t: bfloat16 [1280, 5120], P(None, ('req', 'tok')), may hold values from -0.078125 to 0.078125
- gain_merge: float32 [1280], replicated, may hold values from 0.1 to 1.9
- w_proj: bfloat16 [5120, 4096], P(None, 'tok'), may hold values from -0.078125 to 0.078125
Outputs:
- owned: bfloat16 [8192, 4096], P('req', 'tok')
Inputs may be any that keep to these rules, and one draw needn't show every extreme that they name: `segments`: in each row segment ids start at 0 and never fall; every image covers whole aligned runs of 4 positions and at most 512 positions; image 0 of every row covers exactly 512, and every row holds exactly max(1, 16) + 1 images.
All inputs are finite; a program needn't handle non-finite values.
Results may differ from a plain program's by a relative error of at most 0.015.
The roundings to bfloat16 on the way count: a program that leaves them out, or rounds other values in their place, can miss the bound.
Values may be sent and summed in bfloat16 or wider, within the bound.
No kernel may reach another device: no remote copies, remote signals or barrier semaphores. Data moves between devices by JAX's collectives and lax.ppermute only.
A program may use at most 128 MiB of HBM per device.

v0:
```python
import math

import jax
import jax.numpy as jnp
from jax import lax
from jax.sharding import PartitionSpec as P

HDIM = 80


def layer_norm(values, gain):
    mean = jnp.mean(values, axis=-1, keepdims=True)
    centered = values - mean
    spread = jnp.mean(centered * centered, axis=-1, keepdims=True)
    return centered * lax.rsqrt(spread + 1e-06) * gain


def hidden_fold(rows, pieces):
    up_piece, down_piece = pieces
    hidden = jax.nn.gelu(
        jnp.dot(rows, up_piece, preferred_element_type=jnp.float32), approximate=False
    ).astype(jnp.bfloat16)
    return lax.dot_general(
        hidden, down_piece, (((1,), (1,)), ((), ())), preferred_element_type=jnp.float32
    )


def attend_block(
    queries,
    keys_blocked,
    values_blocked,
    images,
    images_blocked,
    first_row,
    q_block,
    k_block,
    scale,
):
    local_heads = keys_blocked.shape[2]
    query_part = queries[first_row : first_row + q_block].reshape(q_block, local_heads, HDIM)
    query_images = images[first_row : first_row + q_block]
    key_first = jnp.sum((images < images[first_row]).astype(jnp.int32))
    key_last = jnp.sum((images <= images[first_row + q_block - 1]).astype(jnp.int32))
    block_first = key_first // k_block
    block_last = (key_last + k_block - 1) // k_block

    def block_scores(kblock):
        scores = (
            jnp.einsum(
                "qhd,khd->hqk", query_part, keys_blocked[kblock], preferred_element_type=jnp.float32
            )
            * scale
        )
        same = query_images[:, None] == images_blocked[kblock][None, :]
        return jnp.where(same[None], scores, -1e30)

    def scan_stats(kblock, carry):
        row_max, row_sum = carry
        scores = block_scores(kblock)
        new_max = jnp.maximum(row_max, jnp.max(scores, axis=-1))
        row_sum = row_sum * jnp.exp(row_max - new_max) + jnp.sum(
            jnp.exp(scores - new_max[..., None]), axis=-1
        )
        return (new_max, row_sum)

    start_max = jnp.full((local_heads, q_block), -1e30, jnp.float32)
    start_sum = jnp.zeros((local_heads, q_block), jnp.float32)
    row_max, row_sum = lax.fori_loop(block_first, block_last, scan_stats, (start_max, start_sum))

    def add_values(kblock, totals):
        scores = block_scores(kblock)
        weights = (jnp.exp(scores - row_max[..., None]) / row_sum[..., None]).astype(jnp.bfloat16)
        return totals + jnp.einsum(
            "hqk,khd->qhd", weights, values_blocked[kblock], preferred_element_type=jnp.float32
        )

    totals = lax.fori_loop(
        block_first, block_last, add_values, jnp.zeros((q_block, local_heads, HDIM), jnp.float32)
    )
    return totals.reshape(q_block, local_heads * HDIM).astype(jnp.bfloat16)


def per_device(
    tokens, segments, gain_attn, w_qkv, w_out, gain_mlp, w_up, w_down_t, gain_merge, w_proj
):
    inputs = tokens.astype(jnp.float32)
    normed = layer_norm(inputs, gain_attn).astype(jnp.bfloat16)
    local_width = w_qkv.shape[2]
    joined = w_qkv.reshape(w_qkv.shape[0], 3 * local_width)
    stacked = jnp.dot(
        lax.all_gather(normed, "tok", axis=0, tiled=True),
        joined,
        preferred_element_type=jnp.float32,
    ).astype(jnp.bfloat16)
    group = stacked.shape[0]
    local_heads = local_width // HDIM
    q_block = min(512, group)
    k_block = min(128, group)
    scale = 1.0 / math.sqrt(HDIM)
    queries = stacked[:, :local_width]
    keys_blocked = stacked[:, local_width : 2 * local_width].reshape(
        group // k_block, k_block, local_heads, HDIM
    )
    values_blocked = stacked[:, 2 * local_width :].reshape(
        group // k_block, k_block, local_heads, HDIM
    )
    images = segments[0]
    images_blocked = images.reshape(group // k_block, k_block)
    outputs = []
    for block in range(group // q_block):
        outputs.append(
            attend_block(
                queries,
                keys_blocked,
                values_blocked,
                images,
                images_blocked,
                block * q_block,
                q_block,
                k_block,
                scale,
            )
        )
    heads_out = jnp.concatenate(outputs, axis=0)
    attended = lax.psum_scatter(
        jnp.dot(heads_out, w_out, preferred_element_type=jnp.float32).astype(jnp.bfloat16),
        "tok",
        scatter_dimension=0,
        tiled=True,
    ).astype(jnp.float32)
    first = (inputs + attended).astype(jnp.bfloat16)
    normed_mlp = layer_norm(first.astype(jnp.float32), gain_mlp).astype(jnp.bfloat16)
    mlp_out = hidden_fold(
        normed_mlp,
        (
            lax.all_gather(w_up, ("req", "tok"), axis=1, tiled=True),
            lax.all_gather(w_down_t, ("req", "tok"), axis=1, tiled=True),
        ),
    )
    second = first.astype(jnp.float32) + mlp_out
    normed_merge = layer_norm(second, gain_merge).astype(jnp.bfloat16)
    merged = normed_merge.reshape(inputs.shape[0] // 4, 4 * inputs.shape[1])
    projected = jnp.dot(
        lax.all_gather(merged, "tok", axis=0, tiled=True),
        w_proj,
        preferred_element_type=jnp.float32,
    ).astype(jnp.bfloat16)
    return lax.all_to_all(projected, "req", split_axis=0, concat_axis=0, tiled=True)


def solution(mesh):
    return jax.shard_map(
        per_device,
        mesh=mesh,
        in_specs=(
            P(("req", "tok"), None),
            P("req", None),
            P(),
            P(None, None, "tok"),
            P("tok", None),
            P(),
            P(None, ("req", "tok")),
            P(None, ("req", "tok")),
            P(),
            P(None, "tok"),
        ),
        out_specs=P("req", "tok"),
        check_vma=False,
    )
```

profile of v0, /device:TPU:1, one launch (start us, length us, event | category | flops | bytes accessed | tf_op | source)
XLA Modules:
  0.0 347.9 jit_solution(920983166437421868)
XLA Ops:
  7.4 1.4 convert_reduce_fusion.1
  8.8 1.4 fusion.102
  10.2 2.2 fusion.104
  12.5 1.3 fusion.163
  13.8 3.9 %fusion.123 = (s32[]{:T(128)}, s32[]{:T(128)}, s32[]{:T(128)}, s32[]{:T(128)}) fusion(s32[1,1024]{1,0:T(1,128)} %param.19, s32[]{:T(128)} %bitcast.17, s32[]{:T(128)} %bitcast.23, s32[]{:T(128)} %bitcast.16, s32[]{:T(128)} %bitcast.24), kind=kLoop, calls=%fused_computation.156 | loop fusion | flops 12284 | bytes 4128 | tf_op jit(solution)/shard_map/reduce_sum | solution.py:43
  24.0 0.7 fusion.162
  24.7 26.1 %all-gather.5.cloned.1.call-done = bf16[1024,1280]{1,0:T(8,128)(2,1)} async-done(((bf16[256,1280]{1,0:T(8,128)(2,1)}), bf16[1024,1280]{1,0:T(8,128)(2,1)}) %all-gather.5.cloned.1.call-update) | async-done | bytes 2621456 | tf_op jit(solution)/shard_map/all_gather | solution.py:91
  50.8 4.5 %convolution_convert_fusion.1 = bf16[1024,960]{0,1:T(8,128)(2,1)S(1)} fusion(bf16[1024,1280]{1,0:T(8,128)(2,1)} %all-gather.5.cloned.1.call-done, bf16[1280,960]{0,1:T(8,128)(2,1)S(1)} %bitcast.140), kind=kOutput, calls=%fused_computation.126 | convolution fusion | flops 2517565440 | bytes 7045120 | tf_op jit(solution)/shard_map/dot_general | solution.py:90
  55.3 0.9 slice_bitcast_fusion
  56.5 0.7 copy.13
  57.2 1.1 copy.14
  58.3 3.1 while.44
  58.4 0.4 fusion.191
  59.2 0.4 fusion.191
  60.0 0.4 fusion.191
  60.7 0.4 fusion.191
  61.5 0.9 copy.12
  62.5 9.2 %while.45 = (s32[]{:T(128)}, f32[512,4,80]{0,2,1:T(8,128)S(1)}, s32[]{:T(128)}, bf16[8,128,4,80]{1,3,2,0:T(8,128)(2,1)}, s32[512]{0:T(512)S(1)}, /*index=5*/s32[...) while((s32[]{:T(128)}, f32[512,4,80]{0,2,1:T(8,128)S(1)}, ...), condition=%wide.region_9.10_spmd, body=%wide.region_8.9_spmd.sunk | while | flops 85426176 | bytes 2313899 | solution.py:77
  62.7 2.0 fusion.196
  65.0 2.0 fusion.196
  67.3 2.0 fusion.196
  69.6 2.0 fusion.196
  71.8 0.3 copy.18
  72.1 3.1 while.46
  72.3 0.4 fusion.198
  73.0 0.4 fusion.198
  73.8 0.4 fusion.198
  74.5 0.4 fusion.198
  75.2 8.4 %while.47 = (s32[]{:T(128)}, f32[512,4,80]{0,2,1:T(8,128)S(1)}, s32[]{:T(128)}, bf16[8,128,4,80]{1,3,2,0:T(8,128)(2,1)}, s32[512]{0:T(512)S(1)}, /*index=5*/s32[...) while((s32[]{:T(128)}, f32[512,4,80]{0,2,1:T(8,128)S(1)}, ...), condition=%wide.region_17.18_spmd, body=%wide.region_16.17_spmd.sunk | while | flops 85426176 | bytes 2117291 | solution.py:77
  75.5 1.8 fusion.203
  77.6 1.8 fusion.203
  79.7 1.8 fusion.203
  81.8 1.8 fusion.203
  83.7 4.2 %convolution_convert_fusion = bf16[1024,1280]{1,0:T(8,128)(2,1)} fusion(bf16[320,1280]{1,0:T(8,128)(2,1)} %param.22, bf16[512,320]{0,1:T(8,128)(2,1)S(1)} %bitcast.150, bf16[512,320]{0,1:T(8,128)(2,1)S(1)} %bitcast.149), kind=kOutput, calls=%fused_computation.89 | convolution fusion | flops 841482240 | bytes 4096000 | tf_op jit(solution)/shard_map/dot_general | solution.py:126
  88.0 0.5 all-gather.7.cloned.1.call-update
  88.6 0.5 all-gather.9.cloned.1.call-update
  89.4 33.7 %reduce-scatter.2.cloned.1.call-done = bf16[256,1280]{1,0:T(8,128)(2,1)} async-done(((bf16[1024,1280]{1,0:T(8,128)(2,1)}), bf16[256,1280]{1,0:T(8,128)(2,1)}) %reduce-scatter.2.cloned.1.call-update) | async-done | bytes 655376 | tf_op jit(solution)/shard_map/reduce_scatter | solution.py:125
  123.1 1.3 convert_reduce_fusion
  124.4 1.4 fusion.99
  125.9 48.9 %all-gather.7.cloned.1.call-done = bf16[1280,5120]{0,1:T(8,128)(2,1)} async-done(((bf16[1280,40]{0,1:T(8,128)(2,1)}), bf16[1280,5120]{0,1:T(8,128)(2,1)}) %all-gather.7.cloned.1.call-update) | async-done | bytes 13107216 | tf_op jit(solution)/shard_map/all_gather | solution.py:136
  174.8 76.5 %all-gather.9.cloned.1.call-done = bf16[1280,5120]{0,1:T(8,128)(2,1)} async-done(((bf16[1280,40]{0,1:T(8,128)(2,1)}), bf16[1280,5120]{0,1:T(8,128)(2,1)}) %all-gather.9.cloned.1.call-update) | async-done | bytes 13107216 | tf_op jit(solution)/shard_map/all_gather | solution.py:137
  251.3 25.8 %fusion.164 = (f32[256]{0:T(256)S(1)}, f32[256,1280]{1,0:T(8,128)S(1)}) fusion(bf16[1280,5120]{0,1:T(8,128)(2,1)} %all-gather.9.cloned.1.call-done, bf16[1280,5120]{0,1:T(8,128)(2,1)} %all-gather.7.cloned.1.call-done, f32[1280]{0:T(1024)S(1)} %copy-done.6, f32[256]{0:T(256)S(1)} %add_rsqrt_fusion.1, f32[256]{0:T(256)S(1)} %broadcast_multiply_fusion.1, ...), kind=kOutput, calls=%fused_computation.201 | convolution fusion | flops 6801326080 | bytes 28844032 | tf_op jit(solution)/shard_map/dot_general | solution.py:23
  277.1 0.3 multiply_reduce_fusion
  277.7 1.2 reshape.208
  278.9 34.2 %all-gather.11.cloned.1.call-done = bf16[256,5120]{1,0:T(8,128)(2,1)} async-done(((bf16[64,5120]{1,0:T(8,128)(2,1)}), bf16[256,5120]{1,0:T(8,128)(2,1)}) %all-gather.11.cloned.1.call-update) | async-done | bytes 2621456 | tf_op jit(solution)/shard_map/all_gather | solution.py:144
  313.2 7.8 %fusion.106 = bf16[32,8,1024]{2,1,0:T(8,128)(2,1)S(1)} fusion(bf16[256,5120]{1,0:T(8,128)(2,1)} %all-gather.11.cloned.1.call-done, bf16[5120,1024]{1,0:T(8,128)(2,1)} %param.27), kind=kOutput, calls=%fused_computation.141 | convolution fusion | flops 2684616704 | bytes 13631488 | tf_op jit(solution)/shard_map/dot_general | solution.py:143
  321.0 19.1 %all_to_all.12 = bf16[32,8,1024]{2,1,0:T(8,128)(2,1)S(1)} all-to-all(bf16[32,8,1024]{2,1,0:T(8,128)(2,1)S(1)} %fusion.106), channel_id=1, replica_groups=mesh['req'=32,'tok'=4] {'req'}, dimensions={0} | all-to-all | bytes 1048576 | tf_op jit(solution)/shard_map/all_to_all | solution.py:148
  340.0 0.8 copy.76
  (113 shorter events, 5.3 us)
Async XLA Ops:
  7.4 43.4 %copy-start = (bf16[1280,3,320]{0,2,1:T(8,128)(2,1)S(1)}, bf16[1280,3,320]{0,2,1:T(8,128)(2,1)}, u32[]{:S(2)}) copy-start(bf16[1280,3,320]{0,2,1:T(8,128)(2,1)} %param.21) | copy-start | bytes 7372804
  7.4 43.4 %all-gather.5.cloned.1.call-start = ((), (), s32[]{:S(2)}) async-start(), calls=%async_computation.2 | async-start | bytes 3276800 | tf_op jit(solution)/shard_map/all_gather | solution.py:91
  12.4 110.7 %reduce-scatter.2.cloned.1.call-start = ((), (), s32[]{:S(2)}) async-start(), calls=%async_computation.3 | async-start | bytes 3276800 | tf_op jit(solution)/shard_map/reduce_scatter | solution.py:125
  55.2 3.0 copy-start.4
  58.3 3.1 copy-start.3
  83.7 39.4 %copy-start.2 = (bf16[256,1280]{1,0:T(8,128)(2,1)S(1)}, bf16[256,1280]{1,0:T(8,128)(2,1)}, u32[]{:S(2)}) copy-start(bf16[256,1280]{1,0:T(8,128)(2,1)} %param.18) | copy-start | bytes 1966084
  83.7 167.6 %copy-start.6 = (f32[1280]{0:T(1024)S(1)}, f32[1280]{0:T(1024)}, u32[]{:S(2)}) copy-start(f32[1280]{0:T(1024)} %param.23) | copy-start | bytes 15364
  88.0 86.8 %all-gather.7.cloned.1.call-start = ((), (), s32[]{:S(2)}) async-start(), calls=%async_computation.4 | async-start | bytes 13209600 | tf_op jit(solution)/shard_map/all_gather | solution.py:136
  88.6 162.7 %all-gather.9.cloned.1.call-start = ((), (), s32[]{:S(2)}) async-start(), calls=%async_computation.5 | async-start | bytes 13209600 | tf_op jit(solution)/shard_map/all_gather | solution.py:137
  89.2 224.0 %all-gather.11.cloned.1.call-start = ((), (), s32[]{:S(2)}) async-start(), calls=%async_computation.6 | async-start | bytes 3276800 | tf_op jit(solution)/shard_map/all_gather | solution.py:144
  125.9 151.5 %copy-start.5 = (f32[1280]{0:T(1024)S(1)}, f32[1280]{0:T(1024)}, u32[]{:S(2)}) copy-start(f32[1280]{0:T(1024)} %param.26) | copy-start | bytes 15364
  313.2 27.7 %copy-start.1 = (bf16[1280,3,320]{0,2,1:T(8,128)(2,1)S(1)}, bf16[1280,3,320]{0,2,1:T(8,128)(2,1)}, u32[]{:S(2)}) copy-start(bf16[1280,3,320]{0,2,1:T(8,128)(2,1)} %param.21) | copy-start | bytes 7372804
Sparse Core Ops, SparseCore 0:
  12.6 38.1 all-gather.4
  88.1 34.9 reduce-scatter.1
  279.1 34.0 all-gather.10
Sparse Core Ops, SparseCore 1:
  91.4 83.3 all-gather.6
  177.6 73.6 all-gather.8
where the time goes:
time: 349 us; the launch traced here: 348 us
  waiting for transfers between devices  220 us (63%)
  matrix products  61 us (17%)
  between operations  21.1 us (6%)
  blocking collectives  19.1 us (5%)
  other arithmetic  15.7 us (4%)
  local copies, waits for them, and re-layouts  9.17 us (3%)
    all_gather x1, waiting for transfers between devices, per_device(): lax.all_gather(w_down_t, ('req', 'tok'), axis=1, tiled=True)  76.5 us
    all_gather x1, waiting for transfers between devices, per_device(): lax.all_gather(w_up, ('req', 'tok'), axis=1, tiled=True)  48.9 us
    all_gather x1, waiting for transfers between devices, per_device(): lax.all_gather(merged, 'tok', axis=0, tiled=True)  34.2 us
    reduce_scatter x1, waiting for transfers between devices, per_device(): lax.psum_scatter(jnp.dot(heads_out, w_out, preferred_element_type=jnp.flo...  33.7 us
    all_gather x1, waiting for transfers between devices, per_device(): lax.all_gather(normed, 'tok', axis=0, tiled=True)  26.1 us
    dot_general x1, matrix products, hidden_fold(): lax.dot_general(hidden, down_piece, (((1,), (1,)), ((), ())), preferred_e...  25.8 us
    all_to_all x1, blocking collectives, per_device(): lax.all_to_all(projected, 'req', split_axis=0, concat_axis=0, tiled=True)  19.1 us
    dot_general x8, matrix products, add_values(): jnp.einsum('hqk,khd->qhd', weights, values_blocked[kblock], preferred_ele...  15.6 us
  transfers between devices with their start and end apart: 5, of which 5 were waited for; matrix products, arithmetic and copies ran while one was open for 2% of the time, Pallas kernels for 0%

commit v1 on v0

--- a/solution.py
+++ b/solution.py
@@ -3,7 +3,8 @@
 import jax
 import jax.numpy as jnp
 from jax import lax
-from jax.sharding import PartitionSpec as P
+from jax.sharding import Mesh, PartitionSpec as P
+
 
 HDIM = 80
 
@@ -80,9 +81,9 @@
     return totals.reshape(q_block, local_heads * HDIM).astype(jnp.bfloat16)
 
 
-def per_device(
-    tokens, segments, gain_attn, w_qkv, w_out, gain_mlp, w_up, w_down_t, gain_merge, w_proj
-):
+def layer(tokens, segments, gain_attn, w_qkv, w_out, gain_mlp, w_up, w_down_t, gain_merge, w_proj):
+    up_full = lax.all_gather(w_up, ("zx", "tok"), axis=1, tiled=True)
+    down_full = lax.all_gather(w_down_t, ("zx", "tok"), axis=1, tiled=True)
     inputs = tokens.astype(jnp.float32)
     normed = layer_norm(inputs, gain_attn).astype(jnp.bfloat16)
     local_width = w_qkv.shape[2]
@@ -130,12 +131,14 @@
     ).astype(jnp.float32)
     first = (inputs + attended).astype(jnp.bfloat16)
     normed_mlp = layer_norm(first.astype(jnp.float32), gain_mlp).astype(jnp.bfloat16)
-    mlp_out = hidden_fold(
-        normed_mlp,
-        (
-            lax.all_gather(w_up, ("req", "tok"), axis=1, tiled=True),
-            lax.all_gather(w_down_t, ("req", "tok"), axis=1, tiled=True),
+    mlp_out = lax.psum_scatter(
+        hidden_fold(
+            lax.all_gather(normed_mlp, "core", axis=0, tiled=True),
+            (up_full, down_full),
         ),
+        "core",
+        scatter_dimension=0,
+        tiled=True,
     )
     second = first.astype(jnp.float32) + mlp_out
     normed_merge = layer_norm(second, gain_merge).astype(jnp.bfloat16)
@@ -145,25 +148,28 @@
         w_proj,
         preferred_element_type=jnp.float32,
     ).astype(jnp.bfloat16)
-    return lax.all_to_all(projected, "req", split_axis=0, concat_axis=0, tiled=True)
+    return lax.all_to_all(projected, ("zx", "core"), split_axis=0, concat_axis=0, tiled=True)
 
 
 def solution(mesh):
+    devices = mesh.devices
+    split = Mesh(devices.reshape(devices.shape[0] // 2, 2, devices.shape[1]), ("zx", "core", "tok"))
+    rows = ("zx", "core")
     return jax.shard_map(
-        per_device,
-        mesh=mesh,
+        layer,
+        mesh=split,
         in_specs=(
-            P(("req", "tok"), None),
-            P("req", None),
+            P(rows + ("tok",), None),
+            P(rows, None),
             P(),
             P(None, None, "tok"),
             P("tok", None),
             P(),
-            P(None, ("req", "tok")),
-            P(None, ("req", "tok")),
+            P(None, rows + ("tok",)),
+            P(None, rows + ("tok",)),
             P(),
             P(None, "tok"),
         ),
-        out_specs=P("req", "tok"),
+        out_specs=P(rows, "tok"),
         check_vma=False,
     )

time: 349 us -> 432 us (1.24)
  waiting for transfers between devices: 220 us -> 274 us
  local copies, waits for them, and re-layouts: 9.17 us -> 23.9 us
  matrix products: 61 us -> 69.8 us
  other arithmetic: 15.7 us -> 22.9 us
    all_gather x4 -> x5, waiting for transfers between devices: 186 us -> 225 us  [the longest x1 76.3 us: layer(): up_full = lax.all_gather(w_up, ('zx', 'tok'), axis=1, tiled=True)]
    reduce_scatter x1 -> x2, waiting for transfers between devices: 33.7 us -> 47.6 us  [the longest x1 34.3 us: layer(): lax.psum_scatter(jnp.dot(heads_out, w_out, preferred_element_type=jnp.flo...]
    squeeze x8, local copies, waits for them, and re-layouts: 0.44 us -> 7.66 us  [block_scores(): keys_blocked[kblock]]
    dot_general x8, matrix products: 3.15 us -> 10.2 us  [block_scores(): jnp.einsum('qhd,khd->hqk', query_part, keys_blocked[kblock], preferred_el...]
    dot_general x8, matrix products: 15.6 us -> 20 us  [add_values(): jnp.einsum('hqk,khd->qhd', weights, values_blocked[kblock], preferred_ele...]
  transfers between devices with their start and end apart: 5 -> 7, of which waited for: 5 -> 7; matrix products, arithmetic and copies ran while one was open for 2% -> 1% of each run, Pallas kernels for 0% -> 0%
where the time goes in v1:
time: 432 us; the launch traced here: 430 us
  waiting for transfers between devices  274 us (63%)
  matrix products  69.8 us (16%)
  local copies, waits for them, and re-layouts  23.9 us (6%)
  other arithmetic  22.9 us (5%)
  between operations  20 us (5%)
  blocking collectives  19.1 us (4%)
    all_gather x1, waiting for transfers between devices, layer(): up_full = lax.all_gather(w_up, ('zx', 'tok'), axis=1, tiled=True)  76.3 us
    all_gather x1, waiting for transfers between devices, layer(): down_full = lax.all_gather(w_down_t, ('zx', 'tok'), axis=1, tiled=True)  75.1 us
    all_gather x1, waiting for transfers between devices, layer(): lax.all_gather(merged, 'tok', axis=0, tiled=True)  36.3 us
    reduce_scatter x1, waiting for transfers between devices, layer(): lax.psum_scatter(jnp.dot(heads_out, w_out, preferred_element_type=jnp.flo...  34.3 us
    all_gather x1, waiting for transfers between devices, layer(): lax.all_gather(normed, 'tok', axis=0, tiled=True)  26.1 us
    dot_general x1, matrix products, hidden_fold(): lax.dot_general(hidden, down_piece, (((1,), (1,)), ((), ())), preferred_e...  23.1 us
    dot_general x8, matrix products, add_values(): jnp.einsum('hqk,khd->qhd', weights, values_blocked[kblock], preferred_ele...  20 us
    all_to_all x1, blocking collectives, layer(): lax.all_to_all(projected, ('zx', 'core'), split_axis=0, concat_axis=0, ti...  19.1 us
  transfers between devices with their start and end apart: 7, of which 7 were waited for; matrix products, arithmetic and copies ran while one was open for 1% of the time, Pallas kernels for 0%

profile of v1, /device:TPU:1, one launch (start us, length us, event | category | flops | bytes accessed | tf_op | source)
XLA Modules:
  0.0 430.3 jit_solution(11484702749321868855)
XLA Ops:
  6.5 1.4 convert_reduce_fusion.1
  8.0 1.4 fusion.73
  9.4 2.2 fusion.75
  11.7 1.3 fusion.122
  13.0 3.9 fusion.83
  23.9 26.1 %all-gather.6.cloned.1.call-done = bf16[1024,1280]{1,0:T(8,128)(2,1)} async-done(((bf16[256,1280]{1,0:T(8,128)(2,1)}), bf16[1024,1280]{1,0:T(8,128)(2,1)}) %all-gather.6.cloned.1.call-update) | async-done | bytes 2621456 | tf_op jit(solution)/shard_map/all_gather | solution.py:92
  49.9 4.5 %convolution_convert_fusion.1 = bf16[1024,960]{0,1:T(8,128)(2,1)S(1)} fusion(bf16[1024,1280]{1,0:T(8,128)(2,1)} %all-gather.6.cloned.1.call-done, bf16[1280,960]{0,1:T(8,128)(2,1)S(1)} %bitcast.141), kind=kOutput, calls=%fused_computation.97 | convolution fusion | flops 2517565440 | bytes 7045120 | tf_op jit(solution)/shard_map/dot_general | solution.py:91
  57.3 2.9 copy.13
  60.2 1.1 copy.14
  61.3 6.6 %while.44 = (s32[]{:T(128)}, f32[4,512]{1,0:T(4,128)S(1)}, f32[4,512]{1,0:T(4,128)S(1)}, s32[]{:T(128)}, s32[512]{0:T(512)S(1)}, /*index=5*/s32[8,128]{1,0:T(8,1...) while((s32[]{:T(128)}, f32[4,512]{1,0:T(4,128)S(1)}, ...), condition=%wide.region_7.8_spmd, body=%wide.region_4.7_spmd.sunk | while | flops 43323396 | bytes 2748055 | solution.py:69
  61.4 1.3 fusion.150
  63.1 1.3 fusion.150
  64.7 1.3 fusion.150
  66.4 1.3 fusion.150
  67.9 1.2 copy.23
  71.0 16.3 %while.45 = (s32[]{:T(128)}, f32[512,4,80]{0,2,1:T(8,128)}, s32[]{:T(128)}, bf16[8,128,4,80]{1,3,2,0:T(8,128)(2,1)}, s32[512]{0:T(512)S(1)}, /*index=5*/s32[8,12...) while((s32[]{:T(128)}, f32[512,4,80]{0,2,1:T(8,128)}, ...), condition=%wide.region_9.10_spmd, body=%wide.region_8.9_spmd.sunk | while | flops 85426176 | bytes 2313899 | solution.py:78
  72.1 3.0 fusion.155
  76.1 3.0 fusion.155
  80.2 3.0 fusion.155
  84.3 3.0 fusion.155
  87.2 1.9 convert_element_type.73
  89.1 1.1 copy.18
  90.2 6.6 %while.46 = (s32[]{:T(128)}, f32[4,512]{1,0:T(4,128)S(1)}, f32[4,512]{1,0:T(4,128)S(1)}, s32[]{:T(128)}, s32[512]{0:T(512)S(1)}, /*index=5*/s32[8,128]{1,0:T(8,1...) while((s32[]{:T(128)}, f32[4,512]{1,0:T(4,128)S(1)}, ...), condition=%wide.region_15.16_spmd, body=%wide.region_12.15_spmd.sunk | while | flops 43323396 | bytes 2748055 | solution.py:69
  90.3 1.3 fusion.157
  91.9 1.3 fusion.157
  93.6 1.3 fusion.157
  95.2 1.3 fusion.157
  96.8 12.8 %while.47 = (s32[]{:T(128)}, f32[512,4,80]{0,2,1:T(8,128)S(1)}, s32[]{:T(128)}, bf16[8,128,4,80]{1,3,2,0:T(8,128)(2,1)}, s32[512]{0:T(512)S(1)}, /*index=5*/s32[...) while((s32[]{:T(128)}, f32[512,4,80]{0,2,1:T(8,128)S(1)}, ...), condition=%wide.region_17.18_spmd, body=%wide.region_16.17_spmd.sunk | while | flops 85426176 | bytes 2313899 | solution.py:78
  97.9 2.0 fusion.162
  101.1 2.0 fusion.162
  104.3 2.0 fusion.162
  107.5 2.0 fusion.162
  109.7 4.3 %convolution_convert_fusion = bf16[1024,1280]{1,0:T(8,128)(2,1)} fusion(bf16[320,1280]{1,0:T(8,128)(2,1)} %param.22, bf16[512,320]{0,1:T(8,128)(2,1)S(1)} %bitcast.151, bf16[512,320]{0,1:T(8,128)(2,1)} %bitcast.150), kind=kOutput, calls=%fused_computation.89 | convolution fusion | flops 841482240 | bytes 4096000 | tf_op jit(solution)/shard_map/dot_general | solution.py:127
  114.1 34.3 %reduce-scatter.3.cloned.1.call-done = bf16[256,1280]{1,0:T(8,128)(2,1)} async-done(((bf16[1024,1280]{1,0:T(8,128)(2,1)}), bf16[256,1280]{1,0:T(8,128)(2,1)}) %reduce-scatter.3.cloned.1.call-update) | async-done | bytes 655376 | tf_op jit(solution)/shard_map/reduce_scatter | solution.py:126
  148.4 1.6 convert_reduce_fusion
  150.3 1.2 fusion.72
  152.8 11.1 %all-gather.8.cloned.1.call-done = bf16[512,1280]{1,0:T(8,128)(2,1)} async-done(((bf16[256,1280]{1,0:T(8,128)(2,1)}), bf16[512,1280]{1,0:T(8,128)(2,1)}) %all-gather.8.cloned.1.call-update) | async-done | bytes 1310736 | tf_op jit(solution)/shard_map/all_gather | solution.py:136
  163.9 76.3 %all-gather.10.cloned.1.call-done = bf16[1280,2560]{0,1:T(8,128)(2,1)} async-done(((bf16[1280,40]{0,1:T(8,128)(2,1)}), bf16[1280,2560]{0,1:T(8,128)(2,1)}) %all-gather.10.cloned.1.call-update) | async-done | bytes 6553616 | tf_op jit(solution)/shard_map/all_gather | solution.py:85
  240.2 75.1 %all-gather.12.cloned.1.call-done = bf16[1280,2560]{0,1:T(8,128)(2,1)} async-done(((bf16[1280,40]{0,1:T(8,128)(2,1)}), bf16[1280,2560]{0,1:T(8,128)(2,1)}) %all-gather.12.cloned.1.call-update) | async-done | bytes 6553616 | tf_op jit(solution)/shard_map/all_gather | solution.py:86
  315.3 23.1 %fusion.64 = f32[512,1280]{1,0:T(8,128)} fusion(bf16[1280,2560]{0,1:T(8,128)(2,1)} %all-gather.12.cloned.1.call-done, bf16[512,1280]{1,0:T(8,128)(2,1)} %all-gather.8.cloned.1.call-done, bf16[1280,2560]{0,1:T(8,128)(2,1)} %all-gather.10.cloned.1.call-done), kind=kOutput, calls=%fused_computation.90 | convolution fusion | flops 6796083200 | bytes 17039360 | tf_op jit(solution)/shard_map/dot_general | solution.py:24
  338.4 13.3 %reduce-scatter.5.cloned.1.call-done = f32[256,1280]{1,0:T(8,128)} async-done(((f32[512,1280]{1,0:T(8,128)}), f32[256,1280]{1,0:T(8,128)}) %reduce-scatter.5.cloned.1.call-update) | async-done | bytes 1310736 | tf_op jit(solution)/shard_map/reduce_scatter | solution.py:134
  351.7 1.5 fusion.81
  353.3 1.6 multiply_reduce_fusion
  354.9 2.5 multiply_convert_fusion
  357.4 2.3 reshape.208
  359.7 36.3 %all-gather.14.cloned.1.call-done = bf16[256,5120]{1,0:T(8,128)(2,1)} async-done(((bf16[64,5120]{1,0:T(8,128)(2,1)}), bf16[256,5120]{1,0:T(8,128)(2,1)}) %all-gather.14.cloned.1.call-update) | async-done | bytes 2621456 | tf_op jit(solution)/shard_map/all_gather | solution.py:147
  395.9 7.6 %fusion.77 = bf16[32,8,1024]{2,1,0:T(8,128)(2,1)S(1)} fusion(bf16[256,5120]{1,0:T(8,128)(2,1)} %all-gather.14.cloned.1.call-done, bf16[5120,1024]{1,0:T(8,128)(2,1)} %param.27), kind=kOutput, calls=%fused_computation.112 | convolution fusion | flops 2684616704 | bytes 13631488 | tf_op jit(solution)/shard_map/dot_general | solution.py:146
  403.6 19.1 %all_to_all.12 = bf16[32,8,1024]{2,1,0:T(8,128)(2,1)S(1)} all-to-all(bf16[32,8,1024]{2,1,0:T(8,128)(2,1)S(1)} %fusion.77), channel_id=1, replica_groups=mesh['zx'=16,'core'=2,'tok'=4] {'zx','core'}, dimensions={0} | all-to-all | bytes 1048576 | tf_op jit(solution)/shard_map/all_to_all | solution.py:151
  (117 shorter events, 19.5 us)
Async XLA Ops:
  6.5 43.4 %copy-start = (bf16[1280,3,320]{0,2,1:T(8,128)(2,1)S(1)}, bf16[1280,3,320]{0,2,1:T(8,128)(2,1)}, u32[]{:S(2)}) copy-start(bf16[1280,3,320]{0,2,1:T(8,128)(2,1)} %param.21) | copy-start | bytes 7372804
  6.5 43.4 %all-gather.6.cloned.1.call-start = ((), (), s32[]{:S(2)}) async-start(), calls=%async_computation.3 | async-start | bytes 3276800 | tf_op jit(solution)/shard_map/all_gather | solution.py:92
  11.6 136.8 %reduce-scatter.3.cloned.1.call-start = ((), (), s32[]{:S(2)}) async-start(), calls=%async_computation.4 | async-start | bytes 3276800 | tf_op jit(solution)/shard_map/reduce_scatter | solution.py:126
  54.4 6.8 %copy-start.2 = (s32[1,1024]{1,0:T(1,128)S(1)}, s32[1,1024]{1,0:T(1,128)}, u32[]{:S(2)}) copy-start(s32[1,1024]{1,0:T(1,128)} %param.19) | copy-start | bytes 12292
  55.5 0.8 copy-start.1
  109.7 40.6 %copy-start.3 = (f32[1280]{0:T(1024)S(1)}, f32[1280]{0:T(1024)}, u32[]{:S(2)}) copy-start(f32[1280]{0:T(1024)} %param.23) | copy-start | bytes 15364
  114.0 49.9 %all-gather.8.cloned.1.call-start = ((), (), s32[]{:S(2)}) async-start(), calls=%async_computation.5 | async-start | bytes 1966080 | tf_op jit(solution)/shard_map/all_gather | solution.py:136
  151.5 88.7 %all-gather.10.cloned.1.call-start = ((), (), s32[]{:S(2)}) async-start(), calls=%async_computation.6 | async-start | bytes 6656000 | tf_op jit(solution)/shard_map/all_gather | solution.py:85
  152.0 163.2 %all-gather.12.cloned.1.call-start = ((), (), s32[]{:S(2)}) async-start(), calls=%async_computation.7 | async-start | bytes 6656000 | tf_op jit(solution)/shard_map/all_gather | solution.py:86
  152.6 199.1 %reduce-scatter.5.cloned.1.call-start = ((), (), s32[]{:S(2)}) async-start(), calls=%async_computation.8 | async-start | bytes 3932160 | tf_op jit(solution)/shard_map/reduce_scatter | solution.py:134
  338.3 16.6 %copy-start.4 = (f32[1280]{0:T(1024)S(1)}, f32[1280]{0:T(1024)}, u32[]{:S(2)}) copy-start(f32[1280]{0:T(1024)} %param.26) | copy-start | bytes 15364
  338.4 57.6 %all-gather.14.cloned.1.call-start = ((), (), s32[]{:S(2)}) async-start(), calls=%async_computation.9 | async-start | bytes 3276800 | tf_op jit(solution)/shard_map/all_gather | solution.py:147
Sparse Core Ops, SparseCore 0:
  11.7 38.1 all-gather.5
  114.1 34.1 reduce-scatter.2
  151.6 12.3 all-gather.7
  166.7 73.4 all-gather.9
  242.9 72.3 all-gather.11
  338.5 13.1 reduce-scatter.4
  359.8 36.1 all-gather.13

commit v2 on v1

--- a/solution.py
+++ b/solution.py
@@ -14,16 +14,6 @@
     centered = values - mean
     spread = jnp.mean(centered * centered, axis=-1, keepdims=True)
     return centered * lax.rsqrt(spread + 1e-06) * gain
-
-
-def hidden_fold(rows, pieces):
-    up_piece, down_piece = pieces
-    hidden = jax.nn.gelu(
-        jnp.dot(rows, up_piece, preferred_element_type=jnp.float32), approximate=False
-    ).astype(jnp.bfloat16)
-    return lax.dot_general(
-        hidden, down_piece, (((1,), (1,)), ((), ())), preferred_element_type=jnp.float32
-    )
 
 
 def attend_block(
@@ -82,8 +72,14 @@
 
 
 def layer(tokens, segments, gain_attn, w_qkv, w_out, gain_mlp, w_up, w_down_t, gain_merge, w_proj):
-    up_full = lax.all_gather(w_up, ("zx", "tok"), axis=1, tiled=True)
-    down_full = lax.all_gather(w_down_t, ("zx", "tok"), axis=1, tiled=True)
+    every = ("zx", "core", "tok")
+    up_full = lax.all_gather(w_up, every, axis=1, tiled=True)
+    piece = w_down_t.shape[0] // CHUNKS
+    down_parts = []
+    for chunk in range(CHUNKS):
+        down_parts.append(
+            lax.all_gather(w_down_t[chunk * piece : (chunk + 1) * piece], every, axis=1, tiled=True)
+        )
     inputs = tokens.astype(jnp.float32)
     normed = layer_norm(inputs, gain_attn).astype(jnp.bfloat16)
     local_width = w_qkv.shape[2]
@@ -131,16 +127,25 @@
     ).astype(jnp.float32)
     first = (inputs + attended).astype(jnp.bfloat16)
     normed_mlp = layer_norm(first.astype(jnp.float32), gain_mlp).astype(jnp.bfloat16)
-    mlp_out = lax.psum_scatter(
-        hidden_fold(
-            lax.all_gather(normed_mlp, "core", axis=0, tiled=True),
-            (up_full, down_full),
-        ),
-        "core",
-        scatter_dimension=0,
-        tiled=True,
-    )
-    second = first.astype(jnp.float32) + mlp_out
+    hidden = jax.nn.gelu(
+        jnp.dot(normed_mlp, up_full, preferred_element_type=jnp.float32), approximate=False
+    ).astype(jnp.bfloat16)
+    hidden = lax.optimization_barrier(hidden)
+    first_f = first.astype(jnp.float32)
+    pieces = []
+    for chunk in range(CHUNKS):
+        pieces.append(
+            lax.optimization_barrier(
+                first_f[:, chunk * piece : (chunk + 1) * piece]
+                + lax.dot_general(
+                    hidden,
+                    down_parts[chunk],
+                    (((1,), (1,)), ((), ())),
+                    preferred_element_type=jnp.float32,
+                )
+            )
+        )
+    second = jnp.concatenate(pieces, axis=1)
     normed_merge = layer_norm(second, gain_merge).astype(jnp.bfloat16)
     merged = normed_merge.reshape(inputs.shape[0] // 4, 4 * inputs.shape[1])
     projected = jnp.dot(
@@ -149,6 +154,9 @@
         preferred_element_type=jnp.float32,
     ).astype(jnp.bfloat16)
     return lax.all_to_all(projected, ("zx", "core"), split_axis=0, concat_axis=0, tiled=True)
+
+
+CHUNKS = 4
 
 
 def solution(mesh):

time: 432 us -> 521 us (1.21)
  waiting for transfers between devices: 274 us -> 380 us
  local copies, waits for them, and re-layouts: 23.9 us -> 11.4 us
  other arithmetic: 22.9 us -> 16.7 us
    all_gather x3 -> x5, waiting for transfers between devices: 162 us -> 288 us  [the longest x4 238 us: layer(): lax.all_gather(w_down_t[chunk * piece:(chunk + 1) * piece], every, axis=1...]
    reduce_scatter x1 -> x0, waiting for transfers between devices: 13.3 us -> none  [layer(): lax.psum_scatter(hidden_fold(lax.all_gather(normed_mlp, 'core', axis=0, t...]
    dot_general x1 -> x5, matrix products: 23.1 us -> 35 us  [the longest x4 17.8 us: layer(): lax.dot_general(hidden, down_parts[chunk], (((1,), (1,)), ((), ())), pref...]
    squeeze x8, local copies, waits for them, and re-layouts: 7.66 us -> 0.44 us  [block_scores(): keys_blocked[kblock]]
    dot_general x8, matrix products: 10.2 us -> 3.15 us  [block_scores(): jnp.einsum('qhd,khd->hqk', query_part, keys_blocked[kblock], preferred_el...]
    dot_general x8, matrix products: 20 us -> 14.8 us  [add_values(): jnp.einsum('hqk,khd->qhd', weights, values_blocked[kblock], preferred_ele...]
  transfers between devices with their start and end apart: 7 -> 8, of which waited for: 7 -> 8; matrix products, arithmetic and copies ran while one was open for 1% -> 7% of each run, Pallas kernels for 0% -> 0%
where the time goes in v2:
time: 521 us; the launch traced here: 520 us
  waiting for transfers between devices  380 us (73%)
  matrix products  69.5 us (13%)
  between operations  21.5 us (4%)
  blocking collectives  19.1 us (4%)
  other arithmetic  16.7 us (3%)
  local copies, waits for them, and re-layouts  11.4 us (2%)
    all_gather x4, waiting for transfers between devices, layer(): lax.all_gather(w_down_t[chunk * piece:(chunk + 1) * piece], every, axis=1...  238 us
    all_gather x1, waiting for transfers between devices, layer(): up_full = lax.all_gather(w_up, every, axis=1, tiled=True)  49.9 us
    all_gather x1, waiting for transfers between devices, layer(): lax.all_gather(merged, 'tok', axis=0, tiled=True)  32.2 us
    reduce_scatter x1, waiting for transfers between devices, layer(): lax.psum_scatter(jnp.dot(heads_out, w_out, preferred_element_type=jnp.flo...  31.4 us
    all_gather x1, waiting for transfers between devices, layer(): lax.all_gather(normed, 'tok', axis=0, tiled=True)  26.1 us
    all_to_all x1, blocking collectives, layer(): lax.all_to_all(projected, ('zx', 'core'), split_axis=0, concat_axis=0, ti...  19.1 us
    dot_general x4, matrix products, layer(): lax.dot_general(hidden, down_parts[chunk], (((1,), (1,)), ((), ())), pref...  17.8 us
    dot_general x1, matrix products, layer(): jnp.dot(normed_mlp, up_full, preferred_element_type=jnp.float32)  17.2 us
  transfers between devices with their start and end apart: 8, of which 8 were waited for; matrix products, arithmetic and copies ran while one was open for 7% of the time, Pallas kernels for 0%

profile of v2, /device:TPU:1, one launch (start us, length us, event | category | flops | bytes accessed | tf_op | source)
XLA Modules:
  0.0 520.0 jit_solution(1258419832953886196)
XLA Ops:
  7.4 1.4 convert_reduce_fusion
  8.8 1.4 fusion.66
  10.2 2.2 fusion.68
  12.5 1.3 fusion.90
  13.8 3.9 fusion.79
  24.0 0.7 fusion.89
  24.7 26.1 %all-gather.8.cloned.1.call-done = bf16[1024,1280]{1,0:T(8,128)(2,1)} async-done(((bf16[256,1280]{1,0:T(8,128)(2,1)}), bf16[1024,1280]{1,0:T(8,128)(2,1)}) %all-gather.8.cloned.1.call-update) | async-done | bytes 2621456 | tf_op jit(solution)/shard_map/all_gather | solution.py:88
  50.8 4.5 convolution_convert_fusion.1
  55.3 0.9 slice_bitcast_fusion
  56.5 0.7 copy.25
  57.5 3.1 while.44
  60.6 1.2 copy.43
  61.8 0.9 copy.24
  62.8 8.4 %while.45 = (s32[]{:T(128)}, f32[512,4,80]{0,2,1:T(8,128)S(1)}, s32[]{:T(128)}, bf16[8,128,4,80]{1,3,2,0:T(8,128)(2,1)}, s32[512]{0:T(512)S(1)}, /*index=5*/s32[...) while((s32[]{:T(128)}, f32[512,4,80]{0,2,1:T(8,128)S(1)}, ...), condition=%wide.region_9.10_spmd, body=%wide.region_8.9_spmd.sunk | while | flops 85426176 | bytes 2117291 | solution.py:68
  63.1 1.8 fusion.127
  65.2 1.8 fusion.127
  67.3 1.8 fusion.127
  69.4 1.8 fusion.127
  71.2 0.8 convert_element_type.74
  72.4 3.1 while.46
  75.5 8.4 %while.47 = (s32[]{:T(128)}, f32[512,4,80]{0,2,1:T(8,128)S(1)}, s32[]{:T(128)}, bf16[8,128,4,80]{1,3,2,0:T(8,128)(2,1)}, s32[512]{0:T(512)S(1)}, /*index=5*/s32[...) while((s32[]{:T(128)}, f32[512,4,80]{0,2,1:T(8,128)S(1)}, ...), condition=%wide.region_17.18_spmd, body=%wide.region_16.17_spmd.sunk | while | flops 85426176 | bytes 2117291 | solution.py:68
  75.8 1.8 fusion.134
  77.9 1.8 fusion.134
  80.0 1.8 fusion.134
  82.1 1.8 fusion.134
  84.0 4.3 convolution_convert_fusion
  88.4 0.5 all-gather.10.cloned.1.call-update
  89.0 0.7 fusion.88
  90.4 0.7 all-gather.14.cloned.1.call-update
  91.1 0.7 all-gather.12.cloned.1.call-update
  92.1 31.4 %reduce-scatter.2.cloned.1.call-done = bf16[256,1280]{1,0:T(8,128)(2,1)} async-done(((bf16[1024,1280]{1,0:T(8,128)(2,1)}), bf16[256,1280]{1,0:T(8,128)(2,1)}) %reduce-scatter.2.cloned.1.call-update) | async-done | bytes 655376 | tf_op jit(solution)/shard_map/reduce_scatter | solution.py:122
  123.5 1.3 fusion.83
  125.2 49.9 %all-gather.10.cloned.1.call-done = bf16[1280,5120]{0,1:T(8,128)(2,1)} async-done(((bf16[1280,40]{0,1:T(8,128)(2,1)}), bf16[1280,5120]{0,1:T(8,128)(2,1)}) %all-gather.10.cloned.1.call-update) | async-done | bytes 13107216 | tf_op jit(solution)/shard_map/all_gather | solution.py:76
  175.2 17.2 %fusion.56 = bf16[256,5120]{1,0:T(8,128)(2,1)} fusion(bf16[1280,5120]{0,1:T(8,128)(2,1)} %all-gather.10.cloned.1.call-done, bf16[256,1280]{1,0:T(8,128)(2,1)S(1)} %get-tuple-element.354, f32[1280]{0:T(1024)S(1)} %copy-done.8, f32[256]{0:T(256)S(1)} %add_rsqrt_fusion.1, f32[256]{0:T(256)S(1)} %broadcast_multiply_fusion), kind=kOutput, calls=%fused_computation.73 | convolution fusion | flops 3442278400 | bytes 16391168 | tf_op jit(solution)/shard_map/dot_general | solution.py:131
  192.4 51.5 %all-gather.18.cloned.1.call-done = bf16[320,5120]{0,1:T(8,128)(2,1)} async-done(((bf16[320,40]{0,1:T(8,128)(2,1)}), bf16[320,5120]{0,1:T(8,128)(2,1)}) %all-gather.18.cloned.1.call-update) | async-done | bytes 3276816 | tf_op jit(solution)/shard_map/all_gather | solution.py:81
  243.8 4.4 convolution_add_fusion
  248.3 62.2 %all-gather.16.cloned.1.call-done = bf16[320,5120]{0,1:T(8,128)(2,1)} async-done(((bf16[320,40]{0,1:T(8,128)(2,1)}), bf16[320,5120]{0,1:T(8,128)(2,1)}) %all-gather.16.cloned.1.call-update) | async-done | bytes 3276816 | tf_op jit(solution)/shard_map/all_gather | solution.py:81
  310.5 4.4 convolution_add_fusion.1
  314.9 62.4 %all-gather.14.cloned.1.call-done = bf16[320,5120]{0,1:T(8,128)(2,1)} async-done(((bf16[320,40]{0,1:T(8,128)(2,1)}), bf16[320,5120]{0,1:T(8,128)(2,1)}) %all-gather.14.cloned.1.call-update) | async-done | bytes 3276816 | tf_op jit(solution)/shard_map/all_gather | solution.py:81
  377.3 4.5 convolution_add_fusion.2
  381.8 62.3 %all-gather.12.cloned.1.call-done = bf16[320,5120]{0,1:T(8,128)(2,1)} async-done(((bf16[320,40]{0,1:T(8,128)(2,1)}), bf16[320,5120]{0,1:T(8,128)(2,1)}) %all-gather.12.cloned.1.call-update) | async-done | bytes 3276816 | tf_op jit(solution)/shard_map/all_gather | solution.py:81
  444.1 4.5 convolution_add_fusion.3
  448.9 0.8 concatenate.9
  451.7 1.1 multiply_convert_fusion
  452.8 32.2 %all-gather.20.cloned.1.call-done = bf16[256,5120]{1,0:T(8,128)(2,1)} async-done(((bf16[64,5120]{1,0:T(8,128)(2,1)}), bf16[256,5120]{1,0:T(8,128)(2,1)}) %all-gather.20.cloned.1.call-update) | async-done | bytes 2621456 | tf_op jit(solution)/shard_map/all_gather | solution.py:152
  485.0 7.8 %fusion.70 = bf16[32,8,1024]{2,1,0:T(8,128)(2,1)S(1)} fusion(bf16[256,5120]{1,0:T(8,128)(2,1)} %all-gather.20.cloned.1.call-done, bf16[5120,1024]{1,0:T(8,128)(2,1)} %param.27), kind=kOutput, calls=%fused_computation.105 | convolution fusion | flops 2684616704 | bytes 13631488 | tf_op jit(solution)/shard_map/dot_general | solution.py:151
  492.8 19.1 %all_to_all.12 = bf16[32,8,1024]{2,1,0:T(8,128)(2,1)S(1)} all-to-all(bf16[32,8,1024]{2,1,0:T(8,128)(2,1)S(1)} %fusion.70), channel_id=1, replica_groups=mesh['zx'=16,'core'=2,'tok'=4] {'zx','core'}, dimensions={0} | all-to-all | bytes 1048576 | tf_op jit(solution)/shard_map/all_to_all | solution.py:156
  511.9 0.8 copy.102
  (145 shorter events, 12.1 us)
Async XLA Ops:
  7.4 43.4 %copy-start = (bf16[1280,3,320]{0,2,1:T(8,128)(2,1)S(1)}, bf16[1280,3,320]{0,2,1:T(8,128)(2,1)}, u32[]{:S(2)}) copy-start(bf16[1280,3,320]{0,2,1:T(8,128)(2,1)} %param.21) | copy-start | bytes 7372804
  7.4 43.4 %all-gather.8.cloned.1.call-start = ((), (), s32[]{:S(2)}) async-start(), calls=%async_computation.2 | async-start | bytes 3276800 | tf_op jit(solution)/shard_map/all_gather | solution.py:88
  12.4 111.0 %reduce-scatter.2.cloned.1.call-start = ((), (), s32[]{:S(2)}) async-start(), calls=%async_computation.3 | async-start | bytes 3276800 | tf_op jit(solution)/shard_map/reduce_scatter | solution.py:122
  55.2 2.3 copy-start.6
  75.5 8.5 %copy-start.4 = (bf16[512,4,80]{0,2,1:T(8,128)(2,1)S(1)}, bf16[512,4,80]{0,2,1:T(8,128)(2,1)}, u32[]{:S(2)}) copy-start(bf16[512,4,80]{0,2,1:T(8,128)(2,1)} %convert_element_type.74) | copy-start | bytes 983044
  84.0 5.0 copy-start.5
  84.0 8.1 %copy-start.7 = (f32[1280]{0:T(1024)S(1)}, f32[1280]{0:T(1024)}, u32[]{:S(2)}) copy-start(f32[1280]{0:T(1024)} %param.26) | copy-start | bytes 15364
  84.0 39.4 %copy-start.2 = (bf16[256,1280]{1,0:T(8,128)(2,1)S(1)}, bf16[256,1280]{1,0:T(8,128)(2,1)}, u32[]{:S(2)}) copy-start(bf16[256,1280]{1,0:T(8,128)(2,1)} %param.18) | copy-start | bytes 1966084
  88.3 86.8 %copy-start.8 = (f32[1280]{0:T(1024)S(1)}, f32[1280]{0:T(1024)}, u32[]{:S(2)}) copy-start(f32[1280]{0:T(1024)} %param.23) | copy-start | bytes 15364
  88.4 86.8 %all-gather.10.cloned.1.call-start = ((), (), s32[]{:S(2)}) async-start(), calls=%async_computation.4 | async-start | bytes 13209600 | tf_op jit(solution)/shard_map/all_gather | solution.py:76
  89.0 154.9 %all-gather.18.cloned.1.call-start = ((), (), s32[]{:S(2)}) async-start(), calls=%async_computation.8 | async-start | bytes 3962880 | tf_op jit(solution)/shard_map/all_gather | solution.py:81
  89.8 220.7 %all-gather.16.cloned.1.call-start = ((), (), s32[]{:S(2)}) async-start(), calls=%async_computation.7 | async-start | bytes 3962880 | tf_op jit(solution)/shard_map/all_gather | solution.py:81
  90.3 286.9 %all-gather.14.cloned.1.call-start = ((), (), s32[]{:S(2)}) async-start(), calls=%async_computation.6 | async-start | bytes 3962880 | tf_op jit(solution)/shard_map/all_gather | solution.py:81
  91.1 353.0 %all-gather.12.cloned.1.call-start = ((), (), s32[]{:S(2)}) async-start(), calls=%async_computation.5 | async-start | bytes 3962880 | tf_op jit(solution)/shard_map/all_gather | solution.py:81
  91.8 393.2 %all-gather.20.cloned.1.call-start = ((), (), s32[]{:S(2)}) async-start(), calls=%async_computation.9 | async-start | bytes 3276800 | tf_op jit(solution)/shard_map/all_gather | solution.py:152
  124.7 185.8 %copy-start.3 = (f32[256,1280]{1,0:T(8,128)}, f32[256,1280]{1,0:T(8,128)S(1)}, u32[]{:S(2)}) copy-start(f32[256,1280]{1,0:T(8,128)S(1)} %get-tuple-element.353) | copy-start | bytes 3932164
  485.0 27.7 %copy-start.1 = (bf16[1280,3,320]{0,2,1:T(8,128)(2,1)S(1)}, bf16[1280,3,320]{0,2,1:T(8,128)(2,1)}, u32[]{:S(2)}) copy-start(bf16[1280,3,320]{0,2,1:T(8,128)(2,1)} %param.21) | copy-start | bytes 7372804
Sparse Core Ops, SparseCore 0:
  12.6 38.1 all-gather.7
  88.5 34.9 reduce-scatter.1
  453.0 32.0 all-gather.19
Sparse Core Ops, SparseCore 1:
  91.8 83.3 all-gather.9
  178.0 65.8 all-gather.17
  246.7 63.8 all-gather.15
  313.5 63.8 all-gather.13
  380.3 63.8 all-gather.11

commit v3 on v1

--- a/solution.py
+++ b/solution.py
@@ -82,8 +82,8 @@
 
 
 def layer(tokens, segments, gain_attn, w_qkv, w_out, gain_mlp, w_up, w_down_t, gain_merge, w_proj):
-    up_full = lax.all_gather(w_up, ("zx", "tok"), axis=1, tiled=True)
-    down_full = lax.all_gather(w_down_t, ("zx", "tok"), axis=1, tiled=True)
+    both = lax.all_gather(jnp.stack([w_up, w_down_t]), ("zx", "core", "tok"), axis=2, tiled=True)
+    up_full, down_full = both[0], both[1]
     inputs = tokens.astype(jnp.float32)
     normed = layer_norm(inputs, gain_attn).astype(jnp.bfloat16)
     local_width = w_qkv.shape[2]
@@ -131,15 +131,7 @@
     ).astype(jnp.float32)
     first = (inputs + attended).astype(jnp.bfloat16)
     normed_mlp = layer_norm(first.astype(jnp.float32), gain_mlp).astype(jnp.bfloat16)
-    mlp_out = lax.psum_scatter(
-        hidden_fold(
-            lax.all_gather(normed_mlp, "core", axis=0, tiled=True),
-            (up_full, down_full),
-        ),
-        "core",
-        scatter_dimension=0,
-        tiled=True,
-    )
+    mlp_out = hidden_fold(normed_mlp, (up_full, down_full))
     second = first.astype(jnp.float32) + mlp_out
     normed_merge = layer_norm(second, gain_merge).astype(jnp.bfloat16)
     merged = normed_merge.reshape(inputs.shape[0] // 4, 4 * inputs.shape[1])

time: 432 us -> 294 us (0.68)
  waiting for transfers between devices: 274 us -> 165 us
  local copies, waits for them, and re-layouts: 23.9 us -> 9.19 us
  matrix products: 69.8 us -> 61 us
  other arithmetic: 22.9 us -> 16.4 us
    all_gather x3 -> x1, waiting for transfers between devices: 162 us -> 70 us  [layer(): lax.all_gather(jnp.stack([w_up, w_down_t]), ('zx', 'core', 'tok'), axis=2...]
    reduce_scatter x1 -> x0, waiting for transfers between devices: 13.3 us -> none  [layer(): lax.psum_scatter(hidden_fold(lax.all_gather(normed_mlp, 'core', axis=0, t...]
    squeeze x8, local copies, waits for them, and re-layouts: 7.66 us -> 0.44 us  [block_scores(): keys_blocked[kblock]]
    dot_general x8, matrix products: 10.2 us -> 3.15 us  [block_scores(): jnp.einsum('qhd,khd->hqk', query_part, keys_blocked[kblock], preferred_el...]
    dot_general x8, matrix products: 20 us -> 15.6 us  [add_values(): jnp.einsum('hqk,khd->qhd', weights, values_blocked[kblock], preferred_ele...]
  transfers between devices with their start and end apart: 7 -> 4, of which waited for: 7 -> 4; matrix products, arithmetic and copies ran while one was open for 1% -> 3% of each run, Pallas kernels for 0% -> 0%
where the time goes in v3:
time: 294 us; the launch traced here: 293 us
  waiting for transfers between devices  165 us (56%)
  matrix products  61 us (21%)
  between operations  21.1 us (7%)
  blocking collectives  19.1 us (6%)
  other arithmetic  16.4 us (6%)
  local copies, waits for them, and re-layouts  9.19 us (3%)
    all_gather x1, waiting for transfers between devices, layer(): lax.all_gather(jnp.stack([w_up, w_down_t]), ('zx', 'core', 'tok'), axis=2...  70 us
    reduce_scatter x1, waiting for transfers between devices, layer(): lax.psum_scatter(jnp.dot(heads_out, w_out, preferred_element_type=jnp.flo...  34.8 us
    all_gather x1, waiting for transfers between devices, layer(): lax.all_gather(merged, 'tok', axis=0, tiled=True)  34.1 us
    all_gather x1, waiting for transfers between devices, layer(): lax.all_gather(normed, 'tok', axis=0, tiled=True)  26.1 us
    dot_general x1, matrix products, hidden_fold(): lax.dot_general(hidden, down_piece, (((1,), (1,)), ((), ())), preferred_e...  25.8 us
    all_to_all x1, blocking collectives, layer(): lax.all_to_all(projected, ('zx', 'core'), split_axis=0, concat_axis=0, ti...  19.1 us
    dot_general x8, matrix products, add_values(): jnp.einsum('hqk,khd->qhd', weights, values_blocked[kblock], preferred_ele...  15.6 us
    dot_general x1, matrix products, layer(): jnp.dot(lax.all_gather(merged, 'tok', axis=0, tiled=True), w_proj, prefer...  7.78 us
  transfers between devices with their start and end apart: 4, of which 4 were waited for; matrix products, arithmetic and copies ran while one was open for 3% of the time, Pallas kernels for 0%

profile of v3, /device:TPU:1, one launch (start us, length us, event | category | flops | bytes accessed | tf_op | source)
XLA Modules:
  0.0 293.2 jit_solution(14575911120738858815)
XLA Ops:
  7.4 1.4 convert_reduce_fusion.1
  8.8 1.4 fusion.105
  10.2 2.2 fusion.107
  12.5 1.3 fusion.162
  13.8 3.9 %fusion.122 = (s32[]{:T(128)}, s32[]{:T(128)}, s32[]{:T(128)}, s32[]{:T(128)}) fusion(s32[1,1024]{1,0:T(1,128)} %param.19, s32[]{:T(128)} %bitcast.17, s32[]{:T(128)} %bitcast.23, s32[]{:T(128)} %bitcast.16, s32[]{:T(128)} %bitcast.24), kind=kLoop, calls=%fused_computation.160 | loop fusion | flops 12284 | bytes 4128 | tf_op jit(solution)/shard_map/reduce_sum | solution.py:44
  24.0 0.7 fusion.161
  24.7 26.1 %all-gather.4.cloned.1.call-done = bf16[1024,1280]{1,0:T(8,128)(2,1)} async-done(((bf16[256,1280]{1,0:T(8,128)(2,1)}), bf16[1024,1280]{1,0:T(8,128)(2,1)}) %all-gather.4.cloned.1.call-update) | async-done | bytes 2621456 | tf_op jit(solution)/shard_map/all_gather | solution.py:92
  50.8 4.5 %convolution_convert_fusion.1 = bf16[1024,960]{0,1:T(8,128)(2,1)S(1)} fusion(bf16[1024,1280]{1,0:T(8,128)(2,1)} %all-gather.4.cloned.1.call-done, bf16[1280,960]{0,1:T(8,128)(2,1)S(1)} %bitcast.156), kind=kOutput, calls=%fused_computation.130 | convolution fusion | flops 2517565440 | bytes 7045120 | tf_op jit(solution)/shard_map/dot_general | solution.py:91
  55.3 0.9 slice_bitcast_fusion.10
  56.5 0.7 copy.13
  57.2 1.1 copy.14
  58.3 3.1 %while.44 = (s32[]{:T(128)}, f32[4,512]{1,0:T(4,128)S(1)}, f32[4,512]{1,0:T(4,128)S(1)}, s32[]{:T(128)}, s32[512]{0:T(512)S(1)}, /*index=5*/s32[8,128]{1,0:T(8,1...) while((s32[]{:T(128)}, f32[4,512]{1,0:T(4,128)S(1)}, ...), condition=%wide.region_7.8_spmd, body=%wide.region_4.7_spmd.sunk | while | flops 43323396 | bytes 2748055 | solution.py:69
  58.4 0.4 fusion.188
  59.2 0.4 fusion.188
  60.0 0.4 fusion.188
  60.7 0.4 fusion.188
  61.5 0.9 copy.12
  62.5 9.2 %while.45 = (s32[]{:T(128)}, f32[512,4,80]{0,2,1:T(8,128)S(1)}, s32[]{:T(128)}, bf16[8,128,4,80]{1,3,2,0:T(8,128)(2,1)}, s32[512]{0:T(512)S(1)}, /*index=5*/s32[...) while((s32[]{:T(128)}, f32[512,4,80]{0,2,1:T(8,128)S(1)}, ...), condition=%wide.region_9.10_spmd, body=%wide.region_8.9_spmd.sunk | while | flops 85426176 | bytes 2313899 | solution.py:78
  62.7 2.0 fusion.193
  65.0 2.0 fusion.193
  67.3 2.0 fusion.193
  69.6 2.0 fusion.193
  71.8 0.3 copy.18
  72.1 3.1 %while.46 = (s32[]{:T(128)}, f32[4,512]{1,0:T(4,128)S(1)}, f32[4,512]{1,0:T(4,128)S(1)}, s32[]{:T(128)}, s32[512]{0:T(512)S(1)}, /*index=5*/s32[8,128]{1,0:T(8,1...) while((s32[]{:T(128)}, f32[4,512]{1,0:T(4,128)S(1)}, ...), condition=%wide.region_15.16_spmd, body=%wide.region_12.15_spmd.sunk | while | flops 43323396 | bytes 2748055 | solution.py:69
  72.3 0.4 fusion.195
  73.0 0.4 fusion.195
  73.8 0.4 fusion.195
  74.5 0.4 fusion.195
  75.2 8.4 %while.47 = (s32[]{:T(128)}, f32[512,4,80]{0,2,1:T(8,128)S(1)}, s32[]{:T(128)}, bf16[8,128,4,80]{1,3,2,0:T(8,128)(2,1)}, s32[512]{0:T(512)S(1)}, /*index=5*/s32[...) while((s32[]{:T(128)}, f32[512,4,80]{0,2,1:T(8,128)S(1)}, ...), condition=%wide.region_17.18_spmd, body=%wide.region_16.17_spmd.sunk | while | flops 85426176 | bytes 2117291 | solution.py:78
  75.5 1.8 fusion.200
  77.6 1.8 fusion.200
  79.7 1.8 fusion.200
  81.8 1.8 fusion.200
  83.7 4.3 %convolution_convert_fusion = bf16[1024,1280]{1,0:T(8,128)(2,1)} fusion(bf16[320,1280]{1,0:T(8,128)(2,1)} %param.22, bf16[512,320]{0,1:T(8,128)(2,1)S(1)} %bitcast.166, bf16[512,320]{0,1:T(8,128)(2,1)S(1)} %bitcast.165), kind=kOutput, calls=%fused_computation.93 | convolution fusion | flops 841482240 | bytes 4096000 | tf_op jit(solution)/shard_map/dot_general | solution.py:127
  88.1 0.7 pad_maximum_fusion
  88.8 0.2 all-gather.8.cloned.1.call-start
  89.0 34.8 %reduce-scatter.2.cloned.1.call-done = bf16[256,1280]{1,0:T(8,128)(2,1)} async-done(((bf16[1024,1280]{1,0:T(8,128)(2,1)}), bf16[256,1280]{1,0:T(8,128)(2,1)}) %reduce-scatter.2.cloned.1.call-update) | async-done | bytes 655376 | tf_op jit(solution)/shard_map/reduce_scatter | solution.py:126
  123.8 1.3 convert_reduce_fusion
  125.2 1.4 fusion.102
  126.6 70.0 %all-gather.6.cloned.1.call-done = bf16[2,1280,5120]{1,2,0:T(8,128)(2,1)} async-done(((bf16[2,1280,40]{1,2,0:T(8,128)(2,1)}), bf16[2,1280,5120]{1,2,0:T(8,128)(2,1)}) %all-gather.6.cloned.1.call-update) | async-done | bytes 26214416 | tf_op jit(solution)/shard_map/all_gather | solution.py:85
  196.7 25.8 %fusion.163 = (f32[256]{0:T(256)S(1)}, f32[256,1280]{1,0:T(8,128)S(1)}) fusion(bf16[2,1280,5120]{1,2,0:T(8,128)(2,1)} %all-gather.6.cloned.1.call-done, f32[1280]{0:T(1024)S(1)} %copy-done.8, f32[256]{0:T(256)S(1)} %add_rsqrt_fusion.1, f32[256]{0:T(256)S(1)} %broadcast_multiply_fusion.1, bf16[256,1280]{1,0:T(8,128)(2,1)S(1)} %copy-done.2, ...), kind=kOutput, calls=%fused_computation.205 | convolution fusion | flops 6801326080 | bytes 30157824 | tf_op jit(solution)/shard_map/dot_general | solution.py:24
  222.5 0.3 multiply_reduce_fusion
  222.8 0.2 multiply_convert_fusion
  223.1 1.2 reshape.208
  224.3 34.1 %all-gather.8.cloned.1.call-done = bf16[256,5120]{1,0:T(8,128)(2,1)} async-done(((bf16[64,5120]{1,0:T(8,128)(2,1)}), bf16[256,5120]{1,0:T(8,128)(2,1)}) %all-gather.8.cloned.1.call-update) | async-done | bytes 2621456 | tf_op jit(solution)/shard_map/all_gather | solution.py:139
  258.5 7.8 %fusion.109 = bf16[32,8,1024]{2,1,0:T(8,128)(2,1)S(1)} fusion(bf16[256,5120]{1,0:T(8,128)(2,1)} %all-gather.8.cloned.1.call-done, bf16[5120,1024]{1,0:T(8,128)(2,1)} %param.27), kind=kOutput, calls=%fused_computation.145 | convolution fusion | flops 2684616704 | bytes 13631488 | tf_op jit(solution)/shard_map/dot_general | solution.py:138
  266.2 19.1 %all_to_all.12 = bf16[32,8,1024]{2,1,0:T(8,128)(2,1)S(1)} all-to-all(bf16[32,8,1024]{2,1,0:T(8,128)(2,1)S(1)} %fusion.109), channel_id=1, replica_groups=mesh['zx'=16,'core'=2,'tok'=4] {'zx','core'}, dimensions={0} | all-to-all | bytes 1048576 | tf_op jit(solution)/shard_map/all_to_all | solution.py:143
  285.3 0.8 copy.76
  (115 shorter events, 4.8 us)
Async XLA Ops:
  7.4 43.4 %copy-start = (bf16[1280,3,320]{0,2,1:T(8,128)(2,1)S(1)}, bf16[1280,3,320]{0,2,1:T(8,128)(2,1)}, u32[]{:S(2)}) copy-start(bf16[1280,3,320]{0,2,1:T(8,128)(2,1)} %param.21) | copy-start | bytes 7372804
  7.4 43.4 %all-gather.4.cloned.1.call-start = ((), (), s32[]{:S(2)}) async-start(), calls=%async_computation.2 | async-start | bytes 3276800 | tf_op jit(solution)/shard_map/all_gather | solution.py:92
  12.4 111.4 %reduce-scatter.2.cloned.1.call-start = ((), (), s32[]{:S(2)}) async-start(), calls=%async_computation.3 | async-start | bytes 3276800 | tf_op jit(solution)/shard_map/reduce_scatter | solution.py:126
  55.2 3.0 %copy-start.6 = (s32[1,1024]{1,0:T(1,128)S(1)}, s32[1,1024]{1,0:T(1,128)}, u32[]{:S(2)}) copy-start(s32[1,1024]{1,0:T(1,128)} %param.19) | copy-start | bytes 12292
  58.3 3.1 %copy-start.3 = (bf16[40,8,8,128]{3,1,2,0:T(8,128)(2,1)S(1)}, bf16[40,8,8,128]{3,1,2,0:T(8,128)(2,1)}, u32[]{:S(2)}) copy-start(bf16[40,8,8,128]{3,1,2,0:T(8,128)(2,1)} %get-tuple-element.324) | copy-start | bytes 1966084
  83.7 4.4 %copy-start.4 = (bf16[1280,40]{0,1:T(8,128)(2,1)S(1)}, bf16[1280,40]{0,1:T(8,128)(2,1)}, u32[]{:S(2)}) copy-start(bf16[1280,40]{0,1:T(8,128)(2,1)} %param.25) | copy-start | bytes 307204
  83.7 4.4 %copy-start.5 = (bf16[1280,40]{0,1:T(8,128)(2,1)S(1)}, bf16[1280,40]{0,1:T(8,128)(2,1)}, u32[]{:S(2)}) copy-start(bf16[1280,40]{0,1:T(8,128)(2,1)} %param.24) | copy-start | bytes 307204
  83.7 40.1 %copy-start.2 = (bf16[256,1280]{1,0:T(8,128)(2,1)S(1)}, bf16[256,1280]{1,0:T(8,128)(2,1)}, u32[]{:S(2)}) copy-start(bf16[256,1280]{1,0:T(8,128)(2,1)} %param.18) | copy-start | bytes 1966084
  83.7 112.9 %copy-start.8 = (f32[1280]{0:T(1024)S(1)}, f32[1280]{0:T(1024)}, u32[]{:S(2)}) copy-start(f32[1280]{0:T(1024)} %param.23) | copy-start | bytes 15364
  88.0 108.6 %all-gather.6.cloned.1.call-start = ((), (), s32[]{:S(2)}) async-start(), calls=%async_computation.4 | async-start | bytes 26419200 | tf_op jit(solution)/shard_map/all_gather | solution.py:85
  88.8 169.6 %all-gather.8.cloned.1.call-start = ((), (), s32[]{:S(2)}) async-start(), calls=%async_computation.5 | async-start | bytes 3276800 | tf_op jit(solution)/shard_map/all_gather | solution.py:139
  126.6 96.2 %copy-start.7 = (f32[1280]{0:T(1024)S(1)}, f32[1280]{0:T(1024)}, u32[]{:S(2)}) copy-start(f32[1280]{0:T(1024)} %param.26) | copy-start | bytes 15364
  258.5 27.7 %copy-start.1 = (bf16[1280,3,320]{0,2,1:T(8,128)(2,1)S(1)}, bf16[1280,3,320]{0,2,1:T(8,128)(2,1)}, u32[]{:S(2)}) copy-start(bf16[1280,3,320]{0,2,1:T(8,128)(2,1)} %param.21) | copy-start | bytes 7372804
Sparse Core Ops, SparseCore 0:
  12.6 38.1 all-gather.3
  88.1 35.6 reduce-scatter.1
  224.4 33.9 all-gather.7
Sparse Core Ops, SparseCore 1:
  91.5 105.1 all-gather.5

commit v4 on v3

--- a/solution.py
+++ b/solution.py
@@ -24,6 +24,21 @@
     return lax.dot_general(
         hidden, down_piece, (((1,), (1,)), ((), ())), preferred_element_type=jnp.float32
     )
+
+
+def permute_gather(rows, axis):
+    count = lax.axis_size(axis)
+    here = lax.axis_index(axis)
+    shifted = [rows] + [
+        lax.ppermute(rows, axis, [(i, (i + s) % count) for i in range(count)])
+        for s in range(1, count)
+    ]
+    stacked = jnp.stack(shifted)
+    blocks = [
+        lax.dynamic_index_in_dim(stacked, (here - source) % count, axis=0, keepdims=False)
+        for source in range(count)
+    ]
+    return jnp.concatenate(blocks, axis=0)
 
 
 def attend_block(
@@ -89,7 +104,7 @@
     local_width = w_qkv.shape[2]
     joined = w_qkv.reshape(w_qkv.shape[0], 3 * local_width)
     stacked = jnp.dot(
-        lax.all_gather(normed, "tok", axis=0, tiled=True),
+        permute_gather(normed, "tok"),
         joined,
         preferred_element_type=jnp.float32,
     ).astype(jnp.bfloat16)

time: 294 us -> 292 us (level)
  waiting for transfers between devices: 165 us -> 155 us
  starting transfers between devices: 0.31 us -> 6.07 us
  other arithmetic: 16.4 us -> 19.5 us
    all_gather x1 -> x0, waiting for transfers between devices: 26.1 us -> none  [layer(): lax.all_gather(normed, 'tok', axis=0, tiled=True)]
    ppermute x0 -> x3, waiting for transfers between devices: none -> 13.8 us  [permute_gather(): lax.ppermute(rows, axis, [(i, (i + s) % count) for i in range(count)])]
    ppermute x0 -> x3, starting transfers between devices: none -> 5.8 us  [permute_gather(): lax.ppermute(rows, axis, [(i, (i + s) % count) for i in range(count)])]
    another operation x0 -> x2, other arithmetic: none -> 2.98 us  [permute_gather(): stacked = jnp.stack(shifted)]
  transfers between devices with their start and end apart: 4 -> 6, of which waited for: 4 -> 4; matrix products, arithmetic and copies ran while one was open for 3% -> 4% of each run, Pallas kernels for 0% -> 0%
where the time goes in v4:
time: 292 us; the launch traced here: 291 us
  waiting for transfers between devices  155 us (53%)
  matrix products  59.3 us (20%)
  between operations  21.4 us (7%)
  other arithmetic  19.5 us (7%)
  blocking collectives  19.1 us (7%)
  local copies, waits for them, and re-layouts  9.4 us (3%)
  starting transfers between devices  6.07 us (2%)
    all_gather x1, waiting for transfers between devices, layer(): lax.all_gather(jnp.stack([w_up, w_down_t]), ('zx', 'core', 'tok'), axis=2...  70 us
    reduce_scatter x1, waiting for transfers between devices, layer(): lax.psum_scatter(jnp.dot(heads_out, w_out, preferred_element_type=jnp.flo...  37.1 us
    all_gather x1, waiting for transfers between devices, layer(): lax.all_gather(merged, 'tok', axis=0, tiled=True)  34.1 us
    dot_general x1, matrix products, hidden_fold(): lax.dot_general(hidden, down_piece, (((1,), (1,)), ((), ())), preferred_e...  25.8 us
    all_to_all x1, blocking collectives, layer(): lax.all_to_all(projected, ('zx', 'core'), split_axis=0, concat_axis=0, ti...  19.1 us
    dot_general x8, matrix products, add_values(): jnp.einsum('hqk,khd->qhd', weights, values_blocked[kblock], preferred_ele...  15.6 us
    ppermute x3, waiting for transfers between devices, permute_gather(): lax.ppermute(rows, axis, [(i, (i + s) % count) for i in range(count)])  13.8 us
    dot_general x1, matrix products, layer(): jnp.dot(lax.all_gather(merged, 'tok', axis=0, tiled=True), w_proj, prefer...  7.78 us
  transfers between devices with their start and end apart: 6, of which 4 were waited for; matrix products, arithmetic and copies ran while one was open for 4% of the time, Pallas kernels for 0%

profile of v4, /device:TPU:1, one launch (start us, length us, event | category | flops | bytes accessed | tf_op | source)
XLA Modules:
  0.0 290.9 jit_solution(13962455599860928396)
XLA Ops:
  7.4 1.4 convert_reduce_fusion.1
  8.8 1.4 fusion.116
  10.2 2.2 fusion.118
  12.4 2.1 collective-permute-start
  14.5 2.6 collective-permute-start.1
  17.1 1.1 collective-permute-start.2
  18.2 1.4 fusion.174
  19.6 4.0 %fusion.133 = (s32[]{:T(128)}, s32[]{:T(128)}, s32[]{:T(128)}, s32[]{:T(128)}) fusion(s32[1,1024]{1,0:T(1,128)} %param.19, s32[]{:T(128)} %bitcast.17, s32[]{:T(128)} %bitcast.31, s32[]{:T(128)} %bitcast.16, s32[]{:T(128)} %bitcast.32), kind=kLoop, calls=%fused_computation.173 | loop fusion | flops 12284 | bytes 4128 | tf_op jit(solution)/shard_map/reduce_sum | solution.py:59
  29.8 0.7 fusion.173
  30.5 1.4 fusion.184
  31.9 13.8 %collective-permute-done.1 = bf16[256,1280]{1,0:T(8,128)(2,1)} collective-permute-done((bf16[256,1280]{1,0:T(8,128)(2,1)}, bf16[256,1280]{1,0:T(8,128)(2,1)}, u32[]{:S(2)}, u32[]{:S(2)}) %collective-permute-start.1) | collective-permute-done | bytes 655392 | tf_op jit(solution)/shard_map/ppermute | solution.py:33
  45.7 1.6 pad_maximum_fusion
  47.5 2.7 fusion.106
  50.2 0.9 slice_bitcast_fusion.10
  51.4 0.7 copy.13
  52.2 1.1 copy.14
  53.2 3.1 %while.44 = (s32[]{:T(128)}, f32[4,512]{1,0:T(4,128)S(1)}, f32[4,512]{1,0:T(4,128)S(1)}, s32[]{:T(128)}, s32[512]{0:T(512)S(1)}, /*index=5*/s32[8,128]{1,0:T(8,1...) while((s32[]{:T(128)}, f32[4,512]{1,0:T(4,128)S(1)}, ...), condition=%wide.region_7.8_spmd, body=%wide.region_4.7_spmd.sunk | while | flops 43323396 | bytes 2748055 | solution.py:84
  53.4 0.4 fusion.200
  54.2 0.4 fusion.200
  54.9 0.4 fusion.200
  55.7 0.4 fusion.200
  56.4 0.9 copy.12
  57.5 9.2 %while.45 = (s32[]{:T(128)}, f32[512,4,80]{0,2,1:T(8,128)S(1)}, s32[]{:T(128)}, bf16[8,128,4,80]{1,3,2,0:T(8,128)(2,1)}, s32[512]{0:T(512)S(1)}, /*index=5*/s32[...) while((s32[]{:T(128)}, f32[512,4,80]{0,2,1:T(8,128)S(1)}, ...), condition=%wide.region_9.10_spmd, body=%wide.region_8.9_spmd.sunk | while | flops 85426176 | bytes 2313899 | solution.py:93
  57.7 2.0 fusion.205
  60.0 2.0 fusion.205
  62.3 2.0 fusion.205
  64.6 2.0 fusion.205
  67.1 3.1 %while.46 = (s32[]{:T(128)}, f32[4,512]{1,0:T(4,128)S(1)}, f32[4,512]{1,0:T(4,128)S(1)}, s32[]{:T(128)}, s32[512]{0:T(512)S(1)}, /*index=5*/s32[8,128]{1,0:T(8,1...) while((s32[]{:T(128)}, f32[4,512]{1,0:T(4,128)S(1)}, ...), condition=%wide.region_15.16_spmd, body=%wide.region_12.15_spmd.sunk | while | flops 43323396 | bytes 2748055 | solution.py:84
  67.2 0.4 fusion.207
  68.0 0.4 fusion.207
  68.8 0.4 fusion.207
  70.2 8.4 %while.47 = (s32[]{:T(128)}, f32[512,4,80]{0,2,1:T(8,128)S(1)}, s32[]{:T(128)}, bf16[8,128,4,80]{1,3,2,0:T(8,128)(2,1)}, s32[512]{0:T(512)S(1)}, /*index=5*/s32[...) while((s32[]{:T(128)}, f32[512,4,80]{0,2,1:T(8,128)S(1)}, ...), condition=%wide.region_17.18_spmd, body=%wide.region_16.17_spmd.sunk | while | flops 85426176 | bytes 2117291 | solution.py:93
  70.5 1.8 fusion.212
  72.6 1.8 fusion.212
  74.7 1.8 fusion.212
  76.8 1.8 fusion.212
  78.7 4.3 %convolution_convert_fusion = bf16[1024,1280]{1,0:T(8,128)(2,1)} fusion(bf16[320,1280]{1,0:T(8,128)(2,1)} %param.22, bf16[512,320]{0,1:T(8,128)(2,1)S(1)} %bitcast.179, bf16[512,320]{0,1:T(8,128)(2,1)S(1)} %bitcast.178), kind=kOutput, calls=%fused_computation.93 | convolution fusion | flops 841482240 | bytes 4096000 | tf_op jit(solution)/shard_map/dot_general | solution.py:142
  83.1 0.7 pad_maximum_fusion.1
  84.0 37.1 %reduce-scatter.2.cloned.1.call-done = bf16[256,1280]{1,0:T(8,128)(2,1)} async-done(((bf16[1024,1280]{1,0:T(8,128)(2,1)}), bf16[256,1280]{1,0:T(8,128)(2,1)}) %reduce-scatter.2.cloned.1.call-update) | async-done | bytes 655376 | tf_op jit(solution)/shard_map/reduce_scatter | solution.py:141
  121.2 1.3 convert_reduce_fusion
  122.5 1.4 fusion.113
  124.0 70.0 %all-gather.3.cloned.1.call-done = bf16[2,1280,5120]{1,2,0:T(8,128)(2,1)} async-done(((bf16[2,1280,40]{1,2,0:T(8,128)(2,1)}), bf16[2,1280,5120]{1,2,0:T(8,128)(2,1)}) %all-gather.3.cloned.1.call-update) | async-done | bytes 26214416 | tf_op jit(solution)/shard_map/all_gather | solution.py:100
  194.0 25.8 %fusion.175 = (f32[256]{0:T(256)S(1)}, f32[256,1280]{1,0:T(8,128)S(1)}) fusion(bf16[2,1280,5120]{1,2,0:T(8,128)(2,1)} %all-gather.3.cloned.1.call-done, f32[1280]{0:T(1024)S(1)} %copy-done.8, f32[256]{0:T(256)S(1)} %add_rsqrt_fusion.1, f32[256]{0:T(256)S(1)} %broadcast_multiply_fusion.1, bf16[256,1280]{1,0:T(8,128)(2,1)S(1)} %copy-done.2, ...), kind=kOutput, calls=%fused_computation.219 | convolution fusion | flops 6801326080 | bytes 30157824 | tf_op jit(solution)/shard_map/dot_general | solution.py:24
  220.4 1.2 reshape.208
  221.6 34.1 %all-gather.5.cloned.1.call-done = bf16[256,5120]{1,0:T(8,128)(2,1)} async-done(((bf16[64,5120]{1,0:T(8,128)(2,1)}), bf16[256,5120]{1,0:T(8,128)(2,1)}) %all-gather.5.cloned.1.call-update) | async-done | bytes 2621456 | tf_op jit(solution)/shard_map/all_gather | solution.py:154
  255.8 7.8 %fusion.120 = bf16[32,8,1024]{2,1,0:T(8,128)(2,1)S(1)} fusion(bf16[256,5120]{1,0:T(8,128)(2,1)} %all-gather.5.cloned.1.call-done, bf16[5120,1024]{1,0:T(8,128)(2,1)} %param.27), kind=kOutput, calls=%fused_computation.154 | convolution fusion | flops 2684616704 | bytes 13631488 | tf_op jit(solution)/shard_map/dot_general | solution.py:153
  263.6 19.1 %all_to_all.12 = bf16[32,8,1024]{2,1,0:T(8,128)(2,1)S(1)} all-to-all(bf16[32,8,1024]{2,1,0:T(8,128)(2,1)S(1)} %fusion.120), channel_id=1, replica_groups=mesh['zx'=16,'core'=2,'tok'=4] {'zx','core'}, dimensions={0} | all-to-all | bytes 1048576 | tf_op jit(solution)/shard_map/all_to_all | solution.py:158
  282.6 0.8 copy.76
  (121 shorter events, 6.4 us)
Async XLA Ops:
  7.4 40.1 %copy-start = (bf16[1280,3,320]{0,2,1:T(8,128)(2,1)S(1)}, bf16[1280,3,320]{0,2,1:T(8,128)(2,1)}, u32[]{:S(2)}) copy-start(bf16[1280,3,320]{0,2,1:T(8,128)(2,1)} %param.21) | copy-start | bytes 7372804
  7.4 113.8 %reduce-scatter.2.cloned.1.call-start = ((), (), s32[]{:S(2)}) async-start(), calls=%async_computation.2 | async-start | bytes 3276800 | tf_op jit(solution)/shard_map/reduce_scatter | solution.py:141
  12.4 19.5 %collective-permute-start = (bf16[256,1280]{1,0:T(8,128)(2,1)}, bf16[256,1280]{1,0:T(8,128)(2,1)S(1)}, u32[]{:S(2)}, u32[]{:S(2)}) collective-permute-start(bf16[256,1280]{1,0:T(8,128)(2,1)} %fusion.118), channel_id=1, source_target_pairs={{0,1},{1,2},{2,3},{3,0},{4,5},{5,6},{6,7},{7,4},{8,9},{9,10},{10,1... | collective-permute-start | bytes 1966088 | tf_op jit(solution)/shard_map/ppermute | solution.py:33
  14.5 31.1 %collective-permute-start.1 = (bf16[256,1280]{1,0:T(8,128)(2,1)}, bf16[256,1280]{1,0:T(8,128)(2,1)}, u32[]{:S(2)}, u32[]{:S(2)}) collective-permute-start(bf16[256,1280]{1,0:T(8,128)(2,1)} %fusion.118), channel_id=1, source_target_pairs={{0,2},{1,3},{2,0},{3,1},{4,6},{5,7},{6,4},{7,5},{8,10},{9,11},{10,... | collective-permute-start | bytes 1966088 | tf_op jit(solution)/shard_map/ppermute | solution.py:33
  17.1 28.5 %collective-permute-start.2 = (bf16[256,1280]{1,0:T(8,128)(2,1)}, bf16[256,1280]{1,0:T(8,128)(2,1)}, u32[]{:S(2)}, u32[]{:S(2)}) collective-permute-start(bf16[256,1280]{1,0:T(8,128)(2,1)} %fusion.118), channel_id=1, source_target_pairs={{0,3},{1,0},{2,1},{3,2},{4,7},{5,4},{6,5},{7,6},{8,11},{9,8},{10,9... | collective-permute-start | bytes 1966088 | tf_op jit(solution)/shard_map/ppermute | solution.py:33
  50.2 3.0 %copy-start.6 = (s32[1,1024]{1,0:T(1,128)S(1)}, s32[1,1024]{1,0:T(1,128)}, u32[]{:S(2)}) copy-start(s32[1,1024]{1,0:T(1,128)} %param.19) | copy-start | bytes 12292
  53.2 3.1 %copy-start.3 = (bf16[40,8,8,128]{3,1,2,0:T(8,128)(2,1)S(1)}, bf16[40,8,8,128]{3,1,2,0:T(8,128)(2,1)}, u32[]{:S(2)}) copy-start(bf16[40,8,8,128]{3,1,2,0:T(8,128)(2,1)} %get-tuple-element.328) | copy-start | bytes 1966084
  78.7 4.4 %copy-start.4 = (bf16[1280,40]{0,1:T(8,128)(2,1)S(1)}, bf16[1280,40]{0,1:T(8,128)(2,1)}, u32[]{:S(2)}) copy-start(bf16[1280,40]{0,1:T(8,128)(2,1)} %param.25) | copy-start | bytes 307204
  78.7 4.4 %copy-start.5 = (bf16[1280,40]{0,1:T(8,128)(2,1)S(1)}, bf16[1280,40]{0,1:T(8,128)(2,1)}, u32[]{:S(2)}) copy-start(bf16[1280,40]{0,1:T(8,128)(2,1)} %param.24) | copy-start | bytes 307204
  78.7 42.5 %copy-start.2 = (bf16[256,1280]{1,0:T(8,128)(2,1)S(1)}, bf16[256,1280]{1,0:T(8,128)(2,1)}, u32[]{:S(2)}) copy-start(bf16[256,1280]{1,0:T(8,128)(2,1)} %param.18) | copy-start | bytes 1966084
  78.7 115.3 %copy-start.8 = (f32[1280]{0:T(1024)S(1)}, f32[1280]{0:T(1024)}, u32[]{:S(2)}) copy-start(f32[1280]{0:T(1024)} %param.23) | copy-start | bytes 15364
  83.0 111.0 %all-gather.3.cloned.1.call-start = ((), (), s32[]{:S(2)}) async-start(), calls=%async_computation.3 | async-start | bytes 26419200 | tf_op jit(solution)/shard_map/all_gather | solution.py:100
  83.8 172.0 %all-gather.5.cloned.1.call-start = ((), (), s32[]{:S(2)}) async-start(), calls=%async_computation.4 | async-start | bytes 3276800 | tf_op jit(solution)/shard_map/all_gather | solution.py:154
  123.9 96.2 %copy-start.7 = (f32[1280]{0:T(1024)S(1)}, f32[1280]{0:T(1024)}, u32[]{:S(2)}) copy-start(f32[1280]{0:T(1024)} %param.26) | copy-start | bytes 15364
  255.8 27.7 %copy-start.1 = (bf16[1280,3,320]{0,2,1:T(8,128)(2,1)S(1)}, bf16[1280,3,320]{0,2,1:T(8,128)(2,1)}, u32[]{:S(2)}) copy-start(bf16[1280,3,320]{0,2,1:T(8,128)(2,1)} %param.21) | copy-start | bytes 7372804
Sparse Core Ops, SparseCore 0:
  83.1 37.9 reduce-scatter.1
  221.8 33.9 all-gather.4
Sparse Core Ops, SparseCore 1:
  86.5 107.4 all-gather.2
